TPU v7x, 32 devices: a whole 2x2x4 slice. The times are simulated.
32 devices in a mesh: seq: 8 (over y, x, core), panel: 4 (over z).
Axes of the slice: x: 2, y: 2, z: 4, core: 2. Of those that a mesh axis runs over, the one named last changes fastest.
Arguments:
- tokens: bfloat16 [2048, 1024], P('seq', 'panel'), may hold values from -6 to 6
- cotangent: bfloat16 [2048, 1024], P('seq', 'panel'), may hold values from -6 to 6
- in_weight: bfloat16 [3, 1024, 1024], P(None, None, 'panel'), may hold values from -0.1875 to 0.1875
- short_kernel: float32 [3, 3, 1024], P(None, None, 'panel'), may hold values from -1 to 1
- skip_gain: float32 [1024], P('panel'), may hold values from 0.5 to 1.5
- long_filter: float32 [2048, 1024], P('seq', 'panel'), may hold values from -1.25 to 1.25
- out_weight: bfloat16 [1024, 1024], P('panel'), may hold values from -0.1875 to 0.1875
Outputs:
- block_out: bfloat16 [2048, 1024], P('seq', 'panel')
- token_grad: bfloat16 [2048, 1024], P('seq', 'panel')
All inputs are finite; a program needn't handle non-finite values.
Results may differ from a plain program's by a relative error of at most 0.007.
Values may be sent and summed in bfloat16 or wider, within the bound.
No kernel may reach another device: no remote copies, remote signals or barrier semaphores. Data moves between devices by JAX's collectives and lax.ppermute only.
A program may use at most 64 MiB of HBM per device.

v0:
```python
import math
import jax
import jax.numpy as jnp
import numpy as np
from jax import lax
from jax.sharding import PartitionSpec as P

HIGHEST = lax.Precision.HIGHEST
STAGE_A_PRECISION = lax.Precision.HIGH
STAGE_B_PRECISION = lax.Precision.HIGH
WIRE = jnp.bfloat16


def shifted(value, axis, steps):
    count = lax.axis_size(axis)
    initial, last = (max(0, -steps), min(count, count - steps))
    return lax.ppermute(value, axis, [(source, source + steps) for source in range(initial, last)])


def panel_parts(value):
    count = lax.axis_size("panel")
    me = lax.axis_index("panel")
    parts = [(value, me)]
    for k in range(1, count):
        moved = lax.ppermute(value, "panel", [(i, (i + k) % count) for i in range(count)])
        parts.append((moved, (me + count - k) % count))
    return parts


def panel_reduce_scatter(block_of):
    count = lax.axis_size("panel")
    me = lax.axis_index("panel")
    total = block_of(me)
    for k in range(1, count):
        sent = block_of((me + k) % count).astype(jnp.bfloat16)
        total = total + lax.ppermute(
            sent, "panel", [(i, (i + k) % count) for i in range(count)]
        ).astype(jnp.float32)
    return total.astype(jnp.bfloat16)


def phase(numer, period):
    return 2.0 * math.pi / period * (numer % period).astype(jnp.float32)


def transform_tables(shard_count, row_count):
    length = shard_count * row_count
    branch = jnp.arange(2, dtype=jnp.int32)
    shard = jnp.arange(shard_count, dtype=jnp.int32)
    row = jnp.arange(row_count, dtype=jnp.int32)
    small_shard, small_row = (np.arange(shard_count), np.arange(row_count))
    small_branch = np.arange(2)
    theta = (
        -2.0
        * math.pi
        / (2 * shard_count)
        * (
            (
                (2 * small_shard[:, None] * small_shard[None, :])[None]
                + small_branch[:, None, None] * small_shard[None, None, :]
            )
            % (2 * shard_count)
        )
    )
    stage_a_np = np.stack([np.cos(theta), np.sin(theta)], axis=1)
    stage_a = jnp.asarray(stage_a_np, dtype=jnp.float32)
    phi = (
        -2.0
        * math.pi
        / (2 * length)
        * (
            (
                (2 * small_shard[:, None] * small_row[None, :])[None]
                + small_branch[:, None, None] * small_row[None, :][None]
            )
            % (2 * length)
        )
    )
    twiddle = (jnp.asarray(np.cos(phi), jnp.float32), jnp.asarray(np.sin(phi), jnp.float32))
    psi = -phase(row[:, None] * row[None, :], row_count)
    cos_b, sin_b = (jnp.cos(psi), jnp.sin(psi))
    stage_b = jnp.stack([jnp.stack([cos_b, sin_b], axis=1), jnp.stack([-sin_b, cos_b], axis=1)])
    stage_a_inv = jnp.asarray(stage_a_np * (0.5 / length), dtype=jnp.float32)
    return (stage_a, twiddle, stage_b, stage_a_inv)


def complex_scale(value, cos_part, sin_part, axis):
    real_part = lax.index_in_dim(value, 0, axis, keepdims=False)
    imag_part = lax.index_in_dim(value, 1, axis, keepdims=False)
    return jnp.stack(
        [real_part * cos_part - imag_part * sin_part, real_part * sin_part + imag_part * cos_part],
        axis=axis,
    )


def to_columns(rows, wire=jnp.float32):
    shard_count = lax.axis_size("seq")
    batch, row_count, _ = rows.shape
    columns = lax.all_to_all(
        jnp.swapaxes(rows, 1, 2).astype(wire), "seq", split_axis=1, concat_axis=2, tiled=True
    ).astype(jnp.float32)
    return columns.reshape(batch, columns.shape[1], shard_count, row_count)


def to_rows(columns, wire=jnp.float32):
    batch, chan_count, shard_count, row_count = columns.shape
    rows = lax.all_to_all(
        columns.astype(wire), "seq", split_axis=2, concat_axis=1, tiled=True
    ).astype(jnp.float32)
    return jnp.swapaxes(rows.reshape(batch, shard_count * chan_count, row_count), 1, 2)


def forward_spectrum(columns, tables):
    stage_a, twiddle, stage_b, _ = tables
    spread = jnp.einsum("erkp,bcpm->bcerkm", stage_a, columns, precision=STAGE_A_PRECISION)
    spread = complex_scale(spread, twiddle[0], twiddle[1], 3)
    return jnp.einsum("bcerkm,rmsq->bceskq", spread, stage_b, precision=STAGE_B_PRECISION)


def inverse_spectrum(spectrum, tables):
    _, twiddle, stage_b, stage_a_inv = tables
    spread = jnp.einsum("bceskq,rmsq->bcerkm", spectrum, stage_b, precision=STAGE_B_PRECISION)
    spread = complex_scale(spread, twiddle[0], -twiddle[1], 3)
    return jnp.einsum("erkp,bcerkm->bcpm", stage_a_inv, spread, precision=STAGE_A_PRECISION)


def local(tokens, cotangent, in_weight, short_kernel, skip_gain, long_filter, out_weight):
    row_count = tokens.shape[0]
    tap_count = short_kernel.shape[0]
    shard_count = lax.axis_size("seq")
    tables = transform_tables(shard_count, row_count)
    filt_spec = forward_spectrum(to_columns(long_filter[None]), tables)
    width = tokens.shape[1]
    projected = 0.0
    for part, source in panel_parts(tokens):
        projected = projected + jnp.einsum(
            "td,jdc->jtc",
            part,
            lax.dynamic_slice_in_dim(in_weight, source * width, width, axis=1),
            preferred_element_type=jnp.float32,
        )
    grad_gated = 0.0
    for part, source in panel_parts(cotangent):
        grad_gated = grad_gated + lax.dot_general(
            part,
            lax.dynamic_slice_in_dim(out_weight, source * width, width, axis=1),
            (((1,), (1,)), ((), ())),
            preferred_element_type=jnp.float32,
        )
    projected = projected.astype(jnp.bfloat16)
    before = shifted(projected[:, row_count - (tap_count - 1) :, :], "seq", 1)
    extended = jnp.concatenate([before, projected], axis=1).astype(jnp.float32)
    filtered = short_kernel[0][:, None, :] * extended[:, tap_count - 1 :, :]
    for tap_index in range(1, tap_count):
        filtered = (
            filtered
            + short_kernel[tap_index][:, None, :]
            * extended[:, tap_count - 1 - tap_index : tap_count - 1 - tap_index + row_count, :]
        )
    gate_out, gate_in, value_path = (filtered[0], filtered[1], filtered[2])
    signal = value_path * gate_in
    grad_state = grad_gated * gate_out
    spectra = forward_spectrum(to_columns(jnp.stack([signal, grad_state]), WIRE), tables)
    filt_real, filt_imag = (filt_spec[:, :, :, 0], filt_spec[:, :, :, 1])
    sig_real, sig_imag = (spectra[0:1, :, :, 0], spectra[0:1, :, :, 1])
    grad_real, grad_imag = (spectra[1:2, :, :, 0], spectra[1:2, :, :, 1])
    product = jnp.concatenate(
        [
            jnp.stack(
                [
                    sig_real * filt_real - sig_imag * filt_imag,
                    sig_real * filt_imag + sig_imag * filt_real,
                ],
                axis=3,
            ),
            jnp.stack(
                [
                    grad_real * filt_real + grad_imag * filt_imag,
                    grad_imag * filt_real - grad_real * filt_imag,
                ],
                axis=3,
            ),
        ]
    )
    convolved = to_rows(inverse_spectrum(product, tables), WIRE)
    conv_state = convolved[0] + skip_gain[None, :] * signal
    grad_signal = convolved[1] + skip_gain[None, :] * grad_state
    gated_state = (conv_state * gate_out).astype(jnp.bfloat16)
    block_out = panel_reduce_scatter(
        lambda dest: jnp.dot(
            gated_state,
            lax.dynamic_slice_in_dim(out_weight, dest * width, width, axis=1),
            preferred_element_type=jnp.float32,
        )
    )
    grad_gate_out = grad_gated * conv_state
    grad_value = grad_signal * gate_in
    grad_gate_in = grad_signal * value_path
    upstream = jnp.stack([grad_gate_out, grad_gate_in, grad_value])
    after_rim = shifted(upstream[:, : tap_count - 1, :], "seq", -1)
    widened = jnp.concatenate([upstream, after_rim], axis=1)
    grad_projected = short_kernel[0][:, None, :] * widened[:, :row_count, :]
    for tap_index in range(1, tap_count):
        grad_projected = (
            grad_projected
            + short_kernel[tap_index][:, None, :] * widened[:, tap_index : tap_index + row_count, :]
        )
    grad_projected = grad_projected.astype(jnp.bfloat16)
    token_grad = panel_reduce_scatter(
        lambda dest: jnp.einsum(
            "jtc,jdc->td",
            grad_projected,
            lax.dynamic_slice_in_dim(in_weight, dest * width, width, axis=1),
            preferred_element_type=jnp.float32,
        )
    )
    return (block_out, token_grad)


def solution(mesh):
    placed = (
        P("seq", "panel"),
        P("seq", "panel"),
        P(None, None, "panel"),
        P(None, None, "panel"),
        P("panel"),
        P("seq", "panel"),
        P("panel", None),
    )
    return jax.shard_map(
        local,
        mesh=mesh,
        in_specs=placed,
        out_specs=(P("seq", "panel"), P("seq", "panel")),
        check_vma=False,
    )
```

profile of v0, /device:TPU:9, one launch (start us, length us, event | category | flops | bytes accessed | tf_op | source)
XLA Modules:
  0.0 95.5 jit_solution(1160381794692749451)
XLA Ops:
  0.7 1.3 %collective-permute-start = (bf16[256,256]{1,0:T(8,128)(2,1)}, bf16[256,256]{1,0:T(8,128)(2,1)}, u32[]{:S(2)}, u32[]{:S(2)}) collective-permute-start(bf16[256,256]{1,0:T(8,128)(2,1)} %param.11), channel_id=1, source_target_pairs={{0,1},{1,2},{2,3},{3,0},{4,5},{5,6},{6,7},{7,4},{8,9},{9,10},{10,1... | collective-permute-start | bytes 393224 | tf_op jit(solution)/shard_map/ppermute | solution.py:25
  2.2 2.3 %collective-permute-start.1 = (bf16[256,256]{1,0:T(8,128)(2,1)}, bf16[256,256]{1,0:T(8,128)(2,1)}, u32[]{:S(2)}, u32[]{:S(2)}) collective-permute-start(bf16[256,256]{1,0:T(8,128)(2,1)} %param.11), channel_id=1, source_target_pairs={{0,2},{1,3},{2,0},{3,1},{4,6},{5,7},{6,4},{7,5},{8,10},{9,11},{10,... | collective-permute-start | bytes 393224 | tf_op jit(solution)/shard_map/ppermute | solution.py:25
  4.5 1.0 %collective-permute-start.4 = (bf16[256,256]{1,0:T(8,128)(2,1)}, bf16[256,256]{1,0:T(8,128)(2,1)}, u32[]{:S(2)}, u32[]{:S(2)}) collective-permute-start(bf16[256,256]{1,0:T(8,128)(2,1)} %param.12), channel_id=1, source_target_pairs={{0,1},{1,2},{2,3},{3,0},{4,5},{5,6},{6,7},{7,4},{8,9},{9,10},{10,1... | collective-permute-start | bytes 393224 | tf_op jit(solution)/shard_map/ppermute | solution.py:25
  5.5 0.5 collective-permute-start.6
  6.0 1.8 %copy.64 = f32[1,256,256]{1,0,2:T(1,128)} copy(f32[1,256,256]{2,1,0:T(8,128)} %bitcast.216) | data formatting | bytes 524288 | tf_op jit(solution)/shard_map/broadcast_in_dim | solution.py:132
  7.7 5.8 %all-to-all-start.1 = ((f32[1,256,256]{2,0,1:T(1,128)}), f32[1,256,256]{2,0,1:T(1,128)S(1)}, u32[]{:S(2)}, u32[]{:S(2)}) async-start(f32[1,256,256]{2,0,1:T(1,128)} %bitcast.34), calls=%async_computation.1 | async-start | bytes 524288 | tf_op jit(solution)/shard_map/all_to_all | solution.py:99
  13.5 1.0 %fusion.88 = f32[256,1,256]{2,0,1:T(8,128)S(1)} fusion(), kind=kLoop, calls=%fused_computation.124 | loop fusion | flops 1048576 | bytes 262144 | tf_op jit(solution)/shard_map/neg | solution.py:82
  14.5 1.0 %fusion.86 = (f32[256,1,256]{2,0,1:T(8,128)S(1)}, f32[256,1,256]{2,0,1:T(8,128)S(1)}) fusion(), kind=kLoop, calls=%fused_computation.122 | loop fusion | flops 983040 | bytes 524288 | tf_op jit(solution)/shard_map/sin | solution.py:81
  15.6 0.7 slice_bitcast_fusion.5
  16.3 1.9 %fusion.98 = f32[256,256]{0,1:T(8,128)} fusion(bf16[256,256]{1,0:T(8,128)(2,1)} %param.12, bf16[256,1024]{1,0:T(8,128)(2,1)} %param.17, s32[]{:T(128)S(6)} %select_n.85), kind=kOutput, calls=%fused_computation.134 | convolution fusion | flops 33554432 | bytes 524292 | tf_op jit(solution)/shard_map/dot_general | solution.py:144
  18.2 0.3 fusion.51
  18.5 1.1 %maximum_bitcast_fusion.2 = (f32[1,256,2,256]{3,1,0,2:T(8,128)}, f32[1,256,2,256]{3,1,0,2:T(8,128)}) fusion(f32[256,1,256]{2,0,1:T(8,128)S(1)} %get-tuple-element.25, f32[256,1,256]{2,0,1:T(8,128)S(1)} %get-tuple-element.26, f32[256,1,256]{2,0,1:T(8,128)S(1)} %fusion.88), kind=kLoop, calls=%fused_computation.62 | loop fusion | flops 262144 | bytes 1835008 | tf_op jit(solution)/shard_map/stack | solution.py:82
  19.6 0.5 collective-permute-start.5
  20.1 1.2 %convolution_add_fusion.1 = f32[3,256,256]{1,2,0:T(8,128)S(1)} fusion(f32[3,256,256]{1,2,0:T(8,128)S(1)} %fusion.51, bf16[3,1024,256]{2,1,0:T(8,128)(2,1)S(1)} %copy-done, s32[]{:T(128)S(6)} %select_n.87, bf16[256,256]{1,0:T(8,128)(2,1)} %collective-permute-done), kind=kOutput, calls=%fused_computation.19 | convolution fusion | flops 100859904 | bytes 2097156 | tf_op jit(solution)/shard_map/td,jdc->jtc/dot_general | solution.py:136
  21.3 1.2 %fusion.44 = f32[3,256,256]{1,2,0:T(8,128)S(1)} fusion(bf16[3,1024,256]{2,1,0:T(8,128)(2,1)S(1)} %copy-done, s32[]{:T(128)S(6)} %select_n.91, bf16[256,256]{1,0:T(8,128)(2,1)} %collective-permute-done.2), kind=kOutput, calls=%fused_computation.75 | convolution fusion | flops 100663296 | bytes 1310724 | tf_op jit(solution)/shard_map/td,jdc->jtc/dot_general | solution.py:136
  22.6 1.2 %fusion.21 = bf16[3,256,256]{2,1,0:T(8,128)(2,1)S(1)} fusion(f32[3,256,256]{1,2,0:T(8,128)S(1)} %fusion.44, f32[3,256,256]{1,2,0:T(8,128)S(1)} %convolution_add_fusion.1, bf16[3,1024,256]{2,1,0:T(8,128)(2,1)S(1)} %copy-done, s32[]{:T(128)S(6)} %select_n.89, bf16[256,256]{1,0:T(8,128)(2,1)} %collective-permute-done.1), kind=kOutput, calls=%fused_computation.22 | convolution fusion | flops 101253120 | bytes 2490372 | tf_op jit(solution)/shard_map/td,jdc->jtc/dot_general | solution.py:136
  23.8 3.8 %collective-permute-start.3 = (bf16[3,2,256]{2,1,0:T(2,128)(2,1)S(1)}, bf16[3,2,256]{2,1,0:T(2,128)(2,1)S(1)}, u32[]{:S(2)}, u32[]{:S(2)}) collective-permute-start(bf16[3,2,256]{2,1,0:T(2,128)(2,1)S(1)} %slice.111), channel_id=1, source_target_pairs={{0,4},{4,8},{8,12},{12,16},{16,20},{20,24},{24,28},{1,5},{5,9},{9,... | collective-permute-start | bytes 9224 | tf_op jit(solution)/shard_map/ppermute | solution.py:17
  27.6 1.1 %convolution_add_fusion.3 = f32[256,256]{0,1:T(8,128)S(1)} fusion(f32[256,256]{0,1:T(8,128)S(1)} %copy-done.9, bf16[256,256]{1,0:T(8,128)(2,1)} %collective-permute-done.4, bf16[256,1024]{1,0:T(8,128)(2,1)S(1)} %copy-done.7, s32[]{:T(128)S(6)} %select_n.87), kind=kOutput, calls=%fused_computation.31 | convolution fusion | flops 33619968 | bytes 786436 | tf_op jit(solution)/shard_map/dot_general | solution.py:144
  28.8 1.1 %fusion.90 = f32[256,256]{0,1:T(8,128)S(1)} fusion(bf16[256,256]{1,0:T(8,128)(2,1)} %collective-permute-done.6, bf16[256,1024]{1,0:T(8,128)(2,1)S(1)} %copy-done.7, s32[]{:T(128)S(6)} %select_n.91), kind=kOutput, calls=%fused_computation.126 | convolution fusion | flops 33554432 | bytes 524292 | tf_op jit(solution)/shard_map/dot_general | solution.py:144
  29.9 0.2 fusion.26
  30.3 0.2 fusion.41
  30.5 0.4 copy-done.5
  31.1 0.9 copy.34
  31.9 4.2 %all-to-all-start = ((bf16[2,256,256]{2,0,1:T(2,128)(2,1)}), bf16[2,256,256]{2,0,1:T(2,128)(2,1)}, u32[]{:S(2)}, u32[]{:S(2)}) async-start(bf16[2,256,256]{2,0,1:T(2,128)(2,1)} %copy.34), calls=%async_computation | async-start | bytes 524288 | tf_op jit(solution)/shard_map/all_to_all | solution.py:99
  36.1 0.6 convolution_bitcast_fusion.2
  37.0 0.8 copy-done.1
  37.9 1.1 %convolution_bitcast_fusion.1 = f32[1,32,2,2,8,256]{5,1,4,2,0,3:T(8,128)S(1)} fusion(f32[32,2,2,8,256]{4,3,0,2,1:T(8,128)S(1)} %maximum_bitcast_fusion.1, f32[1,256,2,256]{3,1,0,2:T(8,128)S(1)} %copy-done.3, f32[1,256,2,256]{3,1,0,2:T(8,128)S(1)} %copy-done.1), kind=kOutput, calls=%fused_computation.15 | convolution fusion | flops 805568512 | bytes 3145728 | tf_op jit(solution)/shard_map/bcerkm,rmsq->bceskq/dot_general | solution.py:117
  39.1 2.4 %all-to-all-done = bf16[2,256,256]{2,0,1:T(2,128)(2,1)} async-done(((bf16[2,256,256]{2,0,1:T(2,128)(2,1)}), bf16[2,256,256]{2,0,1:T(2,128)(2,1)}, u32[]{:S(2)}, u32[]{:S(2)}) %all-to-all-start) | async-done | bytes 262176 | tf_op jit(solution)/shard_map/all_to_all | solution.py:99
  41.5 1.7 %convolution_bitcast_fusion = f32[2,32,2,2,8,256]{5,4,3,2,1,0:T(8,128)S(1)} fusion(f32[2,2,8,8,1,1]{3,2,1,0,5,4:T(8,128)S(1)} %copy-done.15, bf16[2,8,32,256]{3,0,2,1:T(2,128)(2,1)} %bitcast.18), kind=kOutput, calls=%fused_computation.14 | convolution fusion | flops 25165824 | bytes 2360320 | tf_op jit(solution)/shard_map/erkp,bcpm->bcerkm/dot_general | solution.py:115
  43.2 0.2 multiply_subtract_fusion.1
  43.5 0.2 pad_maximum_fusion
  43.7 0.8 copy-done.2
  44.7 2.7 %fusion.10 = f32[2,32,2,2,8,256]{5,1,4,2,0,3:T(8,128)S(1)} fusion(f32[2,32,2,2,8,256]{5,4,3,2,1,0:T(8,128)S(1)} %pad_maximum_fusion, f32[1,256,2,256]{3,1,0,2:T(8,128)S(1)} %copy-done.4, f32[1,256,2,256]{3,1,0,2:T(8,128)S(1)} %copy-done.2), kind=kOutput, calls=%fused_computation.12 | convolution fusion | flops 1610874880 | bytes 5242880 | tf_op jit(solution)/shard_map/bcerkm,rmsq->bceskq/dot_general | solution.py:117
  47.3 0.5 multiply_subtract_fusion.3
  47.8 0.2 maximum_bitcast_fusion
  48.1 2.7 %fusion.13 = f32[2,32,2,2,8,256]{5,4,3,2,1,0:T(8,128)S(1)} fusion(f32[2,32,2,2,8,256,1]{5,1,4,2,0,3,6:T(8,128)S(1)} %maximum_bitcast_fusion, f32[1,256,2,256]{3,1,0,2:T(8,128)S(1)} %copy-done.4, f32[1,256,2,256]{3,1,0,2:T(8,128)S(1)} %copy-done.2), kind=kOutput, calls=%fused_computation.13 | convolution fusion | flops 1610874880 | bytes 5242880 | tf_op jit(solution)/shard_map/bceskq,rmsq->bcerkm/dot_general | solution.py:122
  50.8 0.3 multiply_subtract_fusion
  51.1 0.4 copy-done.13
  51.5 0.7 fusion.27
  52.2 8.7 %all_to_all.39 = bf16[2,32,8,256]{3,1,0,2:T(8,128)(2,1)S(1)} all-to-all(bf16[2,32,8,256]{3,1,0,2:T(8,128)(2,1)S(1)} %copy.44), channel_id=1, replica_groups=mesh['seq'=8,'panel'=4] {'seq'}, dimensions={2} | all-to-all | bytes 524288 | tf_op jit(solution)/shard_map/all_to_all | solution.py:107
  60.9 0.8 bitcast_convert_fusion
  61.8 1.2 %copy.46 = f32[2,256,256]{1,2,0:T(8,128)S(1)} copy(f32[2,256,256]{2,1,0:T(8,128)} %bitcast.214) | data formatting | bytes 1048576 | tf_op jit(solution)/shard_map/transpose | solution.py:110
  63.2 0.8 copy-done.8
  64.0 0.2 convolution_convert_fusion
  64.2 0.2 convolution_convert_fusion.1
  64.5 3.1 %collective-permute-start.10 = (f32[3,2,256]{2,1,0:T(2,128)S(1)}, f32[3,2,256]{2,1,0:T(2,128)S(1)}, u32[]{:S(2)}, u32[]{:S(2)}) collective-permute-start(f32[3,2,256]{2,1,0:T(2,128)S(1)} %slice.132), channel_id=1, source_target_pairs={{4,0},{8,4},{12,8},{16,12},{20,16},{24,20},{28,24},{5,1},{9,5},{13... | collective-permute-start | bytes 18440 | tf_op jit(solution)/shard_map/ppermute | solution.py:17
  67.7 0.2 convolution_convert_fusion.2
  67.9 2.7 %collective-permute-start.7 = (bf16[256,256]{1,0:T(8,128)(2,1)S(1)}, bf16[256,256]{1,0:T(8,128)(2,1)S(1)}, u32[]{:S(2)}, u32[]{:S(2)}) collective-permute-start(bf16[256,256]{1,0:T(8,128)(2,1)S(1)} %convolution_convert_fusion.2), channel_id=1, source_target_pairs={{0,1},{1,2},{2,3},{3,0},{4,5},{5,6},{6,7},{7,4},{8,9},{9,10},{10,1... | collective-permute-start | bytes 393224 | tf_op jit(solution)/shard_map/ppermute | solution.py:36
  70.6 1.0 %collective-permute-start.8 = (bf16[256,256]{1,0:T(8,128)(2,1)S(1)}, bf16[256,256]{1,0:T(8,128)(2,1)S(1)}, u32[]{:S(2)}, u32[]{:S(2)}) collective-permute-start(bf16[256,256]{1,0:T(8,128)(2,1)S(1)} %convolution_convert_fusion.1), channel_id=1, source_target_pairs={{0,2},{1,3},{2,0},{3,1},{4,6},{5,7},{6,4},{7,5},{8,10},{9,11},{10,... | collective-permute-start | bytes 393224 | tf_op jit(solution)/shard_map/ppermute | solution.py:36
  71.5 0.3 collective-permute-start.9
  71.9 0.3 fusion.39
  72.2 0.3 fusion.31
  72.5 0.3 fusion.30
  72.8 1.2 %collective-permute-start.11 = (bf16[256,256]{1,0:T(8,128)(2,1)S(1)}, bf16[256,256]{1,0:T(8,128)(2,1)S(1)}, u32[]{:S(2)}, u32[]{:S(2)}) collective-permute-start(bf16[256,256]{1,0:T(8,128)(2,1)S(1)} %fusion.30), channel_id=1, source_target_pairs={{0,1},{1,2},{2,3},{3,0},{4,5},{5,6},{6,7},{7,4},{8,9},{9,10},{10,1... | collective-permute-start | bytes 393224 | tf_op jit(solution)/shard_map/ppermute | solution.py:36
  74.0 3.2 %collective-permute-start.12 = (bf16[256,256]{1,0:T(8,128)(2,1)S(1)}, bf16[256,256]{1,0:T(8,128)(2,1)S(1)}, u32[]{:S(2)}, u32[]{:S(2)}) collective-permute-start(bf16[256,256]{1,0:T(8,128)(2,1)S(1)} %fusion.31), channel_id=1, source_target_pairs={{0,2},{1,3},{2,0},{3,1},{4,6},{5,7},{6,4},{7,5},{8,10},{9,11},{10,... | collective-permute-start | bytes 393224 | tf_op jit(solution)/shard_map/ppermute | solution.py:36
  77.2 0.3 fusion.32
  77.5 2.0 %collective-permute-done.7 = bf16[256,256]{1,0:T(8,128)(2,1)S(1)} collective-permute-done((bf16[256,256]{1,0:T(8,128)(2,1)S(1)}, bf16[256,256]{1,0:T(8,128)(2,1)S(1)}, u32[]{:S(2)}, u32[]{:S(2)}) %collective-permute-start.7) | collective-permute-done | bytes 131104 | tf_op jit(solution)/shard_map/ppermute | solution.py:36
  79.5 8.4 %collective-permute-done.8 = bf16[256,256]{1,0:T(8,128)(2,1)S(1)} collective-permute-done((bf16[256,256]{1,0:T(8,128)(2,1)S(1)}, bf16[256,256]{1,0:T(8,128)(2,1)S(1)}, u32[]{:S(2)}, u32[]{:S(2)}) %collective-permute-start.8) | collective-permute-done | bytes 131104 | tf_op jit(solution)/shard_map/ppermute | solution.py:36
  87.9 0.9 collective-permute-done.9
  88.8 0.9 add_convert_fusion
  89.7 1.0 %collective-permute-done.11 = bf16[256,256]{1,0:T(8,128)(2,1)S(1)} collective-permute-done((bf16[256,256]{1,0:T(8,128)(2,1)S(1)}, bf16[256,256]{1,0:T(8,128)(2,1)S(1)}, u32[]{:S(2)}, u32[]{:S(2)}) %collective-permute-start.11) | collective-permute-done | bytes 131104 | tf_op jit(solution)/shard_map/ppermute | solution.py:36
  90.7 2.7 %collective-permute-done.12 = bf16[256,256]{1,0:T(8,128)(2,1)S(1)} collective-permute-done((bf16[256,256]{1,0:T(8,128)(2,1)S(1)}, bf16[256,256]{1,0:T(8,128)(2,1)S(1)}, u32[]{:S(2)}, u32[]{:S(2)}) %collective-permute-start.12) | collective-permute-done | bytes 131104 | tf_op jit(solution)/shard_map/ppermute | solution.py:36
  93.5 1.0 %collective-permute-done.13 = bf16[256,256]{1,0:T(8,128)(2,1)S(1)} collective-permute-done((bf16[256,256]{1,0:T(8,128)(2,1)S(1)}, bf16[256,256]{1,0:T(8,128)(2,1)S(1)}, u32[]{:S(2)}, u32[]{:S(2)}) %collective-permute-start.13) | collective-permute-done | bytes 131104 | tf_op jit(solution)/shard_map/ppermute | solution.py:36
  94.5 1.0 %fusion.62 = bf16[256,256]{1,0:T(8,128)(2,1)} fusion(bf16[3,256,256]{2,1,0:T(8,128)(2,1)S(1)} %fusion.39, bf16[3,1024,256]{2,1,0:T(8,128)(2,1)S(1)} %copy-done, s32[]{:T(128)S(6)} %select_n.85, bf16[256,256]{1,0:T(8,128)(2,1)S(1)} %collective-permute-done.13, bf16[256,256]{1,0:T(8,128)(2,1)S(1)} %collective-permute-done.12, ...), kind=kOutput, calls=%fused_computation.87 | convolution fusion | flops 101122048 | bytes 1310724 | tf_op jit(solution)/shard_map/jtc,jdc->td/dot_general | solution.py:210
  (56 shorter events, 1.4 us)
Async XLA Ops:
  0.6 17.6 %copy-start = (bf16[3,1024,256]{2,1,0:T(8,128)(2,1)S(1)}, bf16[3,1024,256]{2,1,0:T(8,128)(2,1)}, u32[]{:S(2)}) copy-start(bf16[3,1024,256]{2,1,0:T(8,128)(2,1)} %param.13) | copy-start | bytes 4718596
  0.6 17.6 %copy-start.11 = (bf16[256,256]{1,0:T(8,128)(2,1)S(1)}, bf16[256,256]{1,0:T(8,128)(2,1)}, u32[]{:S(2)}) copy-start(bf16[256,256]{1,0:T(8,128)(2,1)} %param.11) | copy-start | bytes 393220
  0.7 18.9 %collective-permute-start = (bf16[256,256]{1,0:T(8,128)(2,1)}, bf16[256,256]{1,0:T(8,128)(2,1)}, u32[]{:S(2)}, u32[]{:S(2)}) collective-permute-start(bf16[256,256]{1,0:T(8,128)(2,1)} %param.11), channel_id=1, source_target_pairs={{0,1},{1,2},{2,3},{3,0},{4,5},{5,6},{6,7},{7,4},{8,9},{9,10},{10,1... | collective-permute-start | bytes 393224 | tf_op jit(solution)/shard_map/ppermute | solution.py:25
  2.0 19.3 %collective-permute-start.2 = (bf16[256,256]{1,0:T(8,128)(2,1)}, bf16[256,256]{1,0:T(8,128)(2,1)}, u32[]{:S(2)}, u32[]{:S(2)}) collective-permute-start(bf16[256,256]{1,0:T(8,128)(2,1)} %param.11), channel_id=1, source_target_pairs={{0,3},{1,0},{2,1},{3,2},{4,7},{5,4},{6,5},{7,6},{8,11},{9,8},{10,9... | collective-permute-start | bytes 393224 | tf_op jit(solution)/shard_map/ppermute | solution.py:25
  2.2 20.4 %collective-permute-start.1 = (bf16[256,256]{1,0:T(8,128)(2,1)}, bf16[256,256]{1,0:T(8,128)(2,1)}, u32[]{:S(2)}, u32[]{:S(2)}) collective-permute-start(bf16[256,256]{1,0:T(8,128)(2,1)} %param.11), channel_id=1, source_target_pairs={{0,2},{1,3},{2,0},{3,1},{4,6},{5,7},{6,4},{7,5},{8,10},{9,11},{10,... | collective-permute-start | bytes 393224 | tf_op jit(solution)/shard_map/ppermute | solution.py:25
  4.5 23.1 %collective-permute-start.4 = (bf16[256,256]{1,0:T(8,128)(2,1)}, bf16[256,256]{1,0:T(8,128)(2,1)}, u32[]{:S(2)}, u32[]{:S(2)}) collective-permute-start(bf16[256,256]{1,0:T(8,128)(2,1)} %param.12), channel_id=1, source_target_pairs={{0,1},{1,2},{2,3},{3,0},{4,5},{5,6},{6,7},{7,4},{8,9},{9,10},{10,1... | collective-permute-start | bytes 393224 | tf_op jit(solution)/shard_map/ppermute | solution.py:25
  5.5 23.3 %collective-permute-start.6 = (bf16[256,256]{1,0:T(8,128)(2,1)}, bf16[256,256]{1,0:T(8,128)(2,1)}, u32[]{:S(2)}, u32[]{:S(2)}) collective-permute-start(bf16[256,256]{1,0:T(8,128)(2,1)} %param.12), channel_id=1, source_target_pairs={{0,3},{1,0},{2,1},{3,2},{4,7},{5,4},{6,5},{7,6},{8,11},{9,8},{10,9... | collective-permute-start | bytes 393224 | tf_op jit(solution)/shard_map/ppermute | solution.py:25
  7.7 24.2 %all-to-all-start.1 = ((f32[1,256,256]{2,0,1:T(1,128)}), f32[1,256,256]{2,0,1:T(1,128)S(1)}, u32[]{:S(2)}, u32[]{:S(2)}) async-start(f32[1,256,256]{2,0,1:T(1,128)} %bitcast.34), calls=%async_computation.1 | async-start | bytes 524288 | tf_op jit(solution)/shard_map/all_to_all | solution.py:99
  19.6 10.3 %collective-permute-start.5 = (bf16[256,256]{1,0:T(8,128)(2,1)}, bf16[256,256]{1,0:T(8,128)(2,1)S(1)}, u32[]{:S(2)}, u32[]{:S(2)}) collective-permute-start(bf16[256,256]{1,0:T(8,128)(2,1)} %param.12), channel_id=1, source_target_pairs={{0,2},{1,3},{2,0},{3,1},{4,6},{5,7},{6,4},{7,5},{8,10},{9,11},{10,... | collective-permute-start | bytes 393224 | tf_op jit(solution)/shard_map/ppermute | solution.py:25
  21.3 6.3 %copy-start.7 = (bf16[256,1024]{1,0:T(8,128)(2,1)S(1)}, bf16[256,1024]{1,0:T(8,128)(2,1)}, u32[]{:S(2)}) copy-start(bf16[256,1024]{1,0:T(8,128)(2,1)} %param.17) | copy-start | bytes 1572868
  21.3 6.3 %copy-start.9 = (f32[256,256]{0,1:T(8,128)S(1)}, f32[256,256]{0,1:T(8,128)}, u32[]{:S(2)}) copy-start(f32[256,256]{0,1:T(8,128)} %fusion.98) | copy-start | bytes 786436
  23.8 6.4 %collective-permute-start.3 = (bf16[3,2,256]{2,1,0:T(2,128)(2,1)S(1)}, bf16[3,2,256]{2,1,0:T(2,128)(2,1)S(1)}, u32[]{:S(2)}, u32[]{:S(2)}) collective-permute-start(bf16[3,2,256]{2,1,0:T(2,128)(2,1)S(1)} %slice.111), channel_id=1, source_target_pairs={{0,4},{4,8},{8,12},{12,16},{16,20},{20,24},{24,28},{1,5},{5,9},{9,... | collective-permute-start | bytes 9224 | tf_op jit(solution)/shard_map/ppermute | solution.py:17
  30.2 0.7 copy-start.5
  30.9 5.2 %copy-start.16 = (f32[2,2,8,8,1]{3,2,4,1,0:T(8,128)S(1)}, f32[2,2,8,8,1]{3,2,4,1,0:T(8,128)}, u32[]{:S(2)}) copy-start(f32[2,2,8,8,1]{3,2,4,1,0:T(8,128)} %constant.93) | copy-start | bytes 3076
  31.0 5.8 %copy-start.10 = (f32[2,8,256]{2,1,0:T(8,128)S(1)}, f32[2,8,256]{2,1,0:T(8,128)}, u32[]{:S(2)}) copy-start(f32[2,8,256]{2,1,0:T(8,128)} %constant.88.clone) | copy-start | bytes 49156
  31.0 5.8 %copy-start.12 = (f32[2,8,256]{2,1,0:T(8,128)S(1)}, f32[2,8,256]{2,1,0:T(8,128)}, u32[]{:S(2)}) copy-start(f32[2,8,256]{2,1,0:T(8,128)} %constant.89.clone) | copy-start | bytes 49156
  31.9 9.6 %all-to-all-start = ((bf16[2,256,256]{2,0,1:T(2,128)(2,1)}), bf16[2,256,256]{2,0,1:T(2,128)(2,1)}, u32[]{:S(2)}, u32[]{:S(2)}) async-start(bf16[2,256,256]{2,0,1:T(2,128)(2,1)} %copy.34), calls=%async_computation | async-start | bytes 524288 | tf_op jit(solution)/shard_map/all_to_all | solution.py:99
  36.7 1.0 %copy-start.1 = (f32[1,256,2,256]{3,1,0,2:T(8,128)S(1)}, f32[1,256,2,256]{3,1,0,2:T(8,128)}, u32[]{:S(2)}) copy-start(f32[1,256,2,256]{3,1,0,2:T(8,128)} %get-tuple-element.20) | copy-start | bytes 1572868
  36.7 1.2 %copy-start.3 = (f32[1,256,2,256]{3,1,0,2:T(8,128)S(1)}, f32[1,256,2,256]{3,1,0,2:T(8,128)}, u32[]{:S(2)}) copy-start(f32[1,256,2,256]{3,1,0,2:T(8,128)} %get-tuple-element.21) | copy-start | bytes 1572868
  37.9 3.5 %copy-start.15 = (f32[2,2,8,8,1,1]{3,2,1,0,5,4:T(8,128)S(1)}, f32[2,2,8,8,1,1]{3,2,1,0,5,4:T(8,128)}, u32[]{:S(2)}) copy-start(f32[2,2,8,8,1,1]{3,2,1,0,5,4:T(8,128)} %constant.92) | copy-start | bytes 3076
  43.5 1.0 %copy-start.2 = (f32[1,256,2,256]{3,1,0,2:T(8,128)S(1)}, f32[1,256,2,256]{3,1,0,2:T(8,128)}, u32[]{:S(2)}) copy-start(f32[1,256,2,256]{3,1,0,2:T(8,128)} %get-tuple-element.20) | copy-start | bytes 1572868
  43.5 1.2 %copy-start.4 = (f32[1,256,2,256]{3,1,0,2:T(8,128)S(1)}, f32[1,256,2,256]{3,1,0,2:T(8,128)}, u32[]{:S(2)}) copy-start(f32[1,256,2,256]{3,1,0,2:T(8,128)} %get-tuple-element.21) | copy-start | bytes 1572868
  48.0 2.7 %copy-start.14 = (f32[2,8,256]{2,1,0:T(8,128)S(1)}, f32[2,8,256]{2,1,0:T(8,128)}, u32[]{:S(2)}) copy-start(f32[2,8,256]{2,1,0:T(8,128)} %constant.91) | copy-start | bytes 49156
  50.8 0.7 copy-start.13
  51.5 11.5 %copy-start.6 = (f32[256,256]{1,0:T(8,128)S(1)}, f32[256,256]{1,0:T(8,128)}, u32[]{:S(2)}) copy-start(f32[256,256]{1,0:T(8,128)} %copy-done.5) | copy-start | bytes 786436
  51.5 11.5 %copy-start.17 = (f32[256]{0:T(256)S(1)}, f32[256]{0:T(256)}, u32[]{:S(2)}) copy-start(f32[256]{0:T(256)} %param.15) | copy-start | bytes 3076
  63.0 1.0 %copy-start.8 = (bf16[256,1024]{1,0:T(8,128)(2,1)S(1)}, bf16[256,1024]{1,0:T(8,128)(2,1)}, u32[]{:S(2)}) copy-start(bf16[256,1024]{1,0:T(8,128)(2,1)} %param.17) | copy-start | bytes 1572868
  64.5 7.3 %collective-permute-start.10 = (f32[3,2,256]{2,1,0:T(2,128)S(1)}, f32[3,2,256]{2,1,0:T(2,128)S(1)}, u32[]{:S(2)}, u32[]{:S(2)}) collective-permute-start(f32[3,2,256]{2,1,0:T(2,128)S(1)} %slice.132), channel_id=1, source_target_pairs={{4,0},{8,4},{12,8},{16,12},{20,16},{24,20},{28,24},{5,1},{9,5},{13... | collective-permute-start | bytes 18440 | tf_op jit(solution)/shard_map/ppermute | solution.py:17
  67.9 11.6 %collective-permute-start.7 = (bf16[256,256]{1,0:T(8,128)(2,1)S(1)}, bf16[256,256]{1,0:T(8,128)(2,1)S(1)}, u32[]{:S(2)}, u32[]{:S(2)}) collective-permute-start(bf16[256,256]{1,0:T(8,128)(2,1)S(1)} %convolution_convert_fusion.2), channel_id=1, source_target_pairs={{0,1},{1,2},{2,3},{3,0},{4,5},{5,6},{6,7},{7,4},{8,9},{9,10},{10,1... | collective-permute-start | bytes 393224 | tf_op jit(solution)/shard_map/ppermute | solution.py:36
  70.6 17.4 %collective-permute-start.8 = (bf16[256,256]{1,0:T(8,128)(2,1)S(1)}, bf16[256,256]{1,0:T(8,128)(2,1)S(1)}, u32[]{:S(2)}, u32[]{:S(2)}) collective-permute-start(bf16[256,256]{1,0:T(8,128)(2,1)S(1)} %convolution_convert_fusion.1), channel_id=1, source_target_pairs={{0,2},{1,3},{2,0},{3,1},{4,6},{5,7},{6,4},{7,5},{8,10},{9,11},{10,... | collective-permute-start | bytes 393224 | tf_op jit(solution)/shard_map/ppermute | solution.py:36
  71.5 17.3 %collective-permute-start.9 = (bf16[256,256]{1,0:T(8,128)(2,1)S(1)}, bf16[256,256]{1,0:T(8,128)(2,1)S(1)}, u32[]{:S(2)}, u32[]{:S(2)}) collective-permute-start(bf16[256,256]{1,0:T(8,128)(2,1)S(1)} %convolution_convert_fusion), channel_id=1, source_target_pairs={{0,3},{1,0},{2,1},{3,2},{4,7},{5,4},{6,5},{7,6},{8,11},{9,8},{10,9... | collective-permute-start | bytes 393224 | tf_op jit(solution)/shard_map/ppermute | solution.py:36
  72.8 17.9 %collective-permute-start.11 = (bf16[256,256]{1,0:T(8,128)(2,1)S(1)}, bf16[256,256]{1,0:T(8,128)(2,1)S(1)}, u32[]{:S(2)}, u32[]{:S(2)}) collective-permute-start(bf16[256,256]{1,0:T(8,128)(2,1)S(1)} %fusion.30), channel_id=1, source_target_pairs={{0,1},{1,2},{2,3},{3,0},{4,5},{5,6},{6,7},{7,4},{8,9},{9,10},{10,1... | collective-permute-start | bytes 393224 | tf_op jit(solution)/shard_map/ppermute | solution.py:36
  74.0 19.4 %collective-permute-start.12 = (bf16[256,256]{1,0:T(8,128)(2,1)S(1)}, bf16[256,256]{1,0:T(8,128)(2,1)S(1)}, u32[]{:S(2)}, u32[]{:S(2)}) collective-permute-start(bf16[256,256]{1,0:T(8,128)(2,1)S(1)} %fusion.31), channel_id=1, source_target_pairs={{0,2},{1,3},{2,0},{3,1},{4,6},{5,7},{6,4},{7,5},{8,10},{9,11},{10,... | collective-permute-start | bytes 393224 | tf_op jit(solution)/shard_map/ppermute | solution.py:36
  79.5 15.0 %collective-permute-start.13 = (bf16[256,256]{1,0:T(8,128)(2,1)S(1)}, bf16[256,256]{1,0:T(8,128)(2,1)S(1)}, u32[]{:S(2)}, u32[]{:S(2)}) collective-permute-start(bf16[256,256]{1,0:T(8,128)(2,1)S(1)} %fusion.32), channel_id=1, source_target_pairs={{0,3},{1,0},{2,1},{3,2},{4,7},{5,4},{6,5},{7,6},{8,11},{9,8},{10,9... | collective-permute-start | bytes 393224 | tf_op jit(solution)/shard_map/ppermute | solution.py:36
where the time goes:
time: 96.3 us; the launch traced here: 95.5 us
  starting transfers between devices  31.1 us (32%)
  matrix products  21.1 us (22%)
  waiting for transfers between devices  18.5 us (19%)
  blocking collectives  8.7 us (9%)
  local copies, waits for them, and re-layouts  8.3 us (9%)
  other arithmetic  6.54 us (7%)
  between operations  1.23 us (1%)
    ppermute x6, waiting for transfers between devices, panel_reduce_scatter(): lax.ppermute(sent, 'panel', [(i, (i + k) % count) for i in range(count)])  16.1 us
    all_to_all x2, starting transfers between devices, to_columns(): lax.all_to_all(jnp.swapaxes(rows, 1, 2).astype(wire), 'seq', split_axis=1...  9.98 us
    all_to_all x1, blocking collectives, to_rows(): lax.all_to_all(columns.astype(wire), 'seq', split_axis=2, concat_axis=1,...  8.7 us
    ppermute x6, starting transfers between devices, panel_reduce_scatter(): lax.ppermute(sent, 'panel', [(i, (i + k) % count) for i in range(count)])  8.36 us
    ppermute x2, starting transfers between devices, shifted(): lax.ppermute(value, axis, [(source, source + steps) for source in range(i...  6.95 us
    ppermute x6, starting transfers between devices, panel_parts(): lax.ppermute(value, 'panel', [(i, (i + k) % count) for i in range(count)])  5.8 us
    dot_general x4, matrix products, local(): lax.dot_general(part, lax.dynamic_slice_in_dim(out_weight, source * width...  4.43 us
    dot_general x4, matrix products, local(): jnp.einsum('td,jdc->jtc', part, lax.dynamic_slice_in_dim(in_weight, sourc...  3.86 us
  transfers between devices with their start and end apart: 16, of which 7 were waited for; matrix products, arithmetic and copies ran while one was open for 20% of the time, Pallas kernels for 0%

commit v1 on v0

--- a/solution.py
+++ b/solution.py
@@ -9,6 +9,28 @@
 STAGE_A_PRECISION = lax.Precision.HIGH
 STAGE_B_PRECISION = lax.Precision.HIGH
 WIRE = jnp.bfloat16
+
+
+def in_blocks(x, dim, devices):
+    before, after = (x.shape[:dim], x.shape[dim + 1 :])
+    return jnp.moveaxis(x.reshape(*before, devices, -1, *after), dim, 0)
+
+
+def joined_along(pieces, dim):
+    pieces = jnp.moveaxis(pieces, 0, dim)
+    dims = pieces.shape
+    return pieces.reshape(*dims[:dim], dims[dim] * dims[dim + 1], *dims[dim + 2 :])
+
+
+def swapped_with_each(x, axis, split_dim, concat_dim):
+    size, index = (lax.axis_size(axis), lax.axis_index(axis))
+    tiles = in_blocks(x, split_dim, size)
+    done = [tiles[index]]
+    for lap in range(1, size):
+        sent = tiles[index ^ lap]
+        done.append(lax.ppermute(sent, axis, [(i, i ^ lap) for i in range(size)]))
+    tiles = jnp.stack(done)[index ^ jnp.arange(size)]
+    return joined_along(tiles, concat_dim)
 
 
 def shifted(value, axis, steps):
@@ -96,9 +118,9 @@
 def to_columns(rows, wire=jnp.float32):
     shard_count = lax.axis_size("seq")
     batch, row_count, _ = rows.shape
-    columns = lax.all_to_all(
-        jnp.swapaxes(rows, 1, 2).astype(wire), "seq", split_axis=1, concat_axis=2, tiled=True
-    ).astype(jnp.float32)
+    columns = swapped_with_each(jnp.swapaxes(rows, 1, 2).astype(wire), "seq", 1, 2).astype(
+        jnp.float32
+    )
     return columns.reshape(batch, columns.shape[1], shard_count, row_count)
 
 

time: 96.3 us -> 133 us (1.38)
  starting transfers between devices: 31.1 us -> 43.6 us
  local copies, waits for them, and re-layouts: 8.3 us -> 19 us
  waiting for transfers between devices: 18.5 us -> 29.2 us
  other arithmetic: 6.54 us -> 8.48 us
    ppermute x0 -> x14, starting transfers between devices: none -> 22 us  [swapped_with_each(): done.append(lax.ppermute(sent, axis, [(i, i ^ lap) for i in range(size)]))]
    ppermute x0 -> x14, waiting for transfers between devices: none -> 13.2 us  [swapped_with_each(): done.append(lax.ppermute(sent, axis, [(i, i ^ lap) for i in range(size)]))]
    all_to_all x2 -> x0, starting transfers between devices: 9.98 us -> none  [to_columns(): lax.all_to_all(jnp.swapaxes(rows, 1, 2).astype(wire), 'seq', split_axis=1...]
    unnamed x37 -> x68, local copies, waits for them, and re-layouts: 3.63 us -> 10.2 us
    gather x0 -> x2, local copies, waits for them, and re-layouts: none -> 2.91 us  [swapped_with_each(): tiles = jnp.stack(done)[index ^ jnp.arange(size)]]
    all_to_all x2 -> x0, waiting for transfers between devices: 2.4 us -> none  [to_columns(): lax.all_to_all(jnp.swapaxes(rows, 1, 2).astype(wire), 'seq', split_axis=1...]
    broadcast_in_dim x1 -> x0, local copies, waits for them, and re-layouts: 1.79 us -> none  [local(): filt_spec = forward_spectrum(to_columns(long_filter[None]), tables)]
  transfers between devices with their start and end apart: 16 -> 28, of which waited for: 7 -> 14; matrix products, arithmetic and copies ran while one was open for 20% -> 20% of each run, Pallas kernels for 0% -> 0%
where the time goes in v1:
time: 133 us; the launch traced here: 132 us
  starting transfers between devices  43.6 us (33%)
  waiting for transfers between devices  29.2 us (22%)
  matrix products  21.4 us (16%)
  local copies, waits for them, and re-layouts  19 us (14%)
  blocking collectives  8.76 us (7%)
  other arithmetic  8.48 us (6%)
  between operations  1.38 us (1%)
    ppermute x14, starting transfers between devices, swapped_with_each(): done.append(lax.ppermute(sent, axis, [(i, i ^ lap) for i in range(size)]))  22 us
    ppermute x6, waiting for transfers between devices, panel_reduce_scatter(): lax.ppermute(sent, 'panel', [(i, (i + k) % count) for i in range(count)])  16 us
    ppermute x14, waiting for transfers between devices, swapped_with_each(): done.append(lax.ppermute(sent, axis, [(i, i ^ lap) for i in range(size)]))  13.2 us
    unnamed x68, local copies, waits for them, and re-layouts  10.2 us
    all_to_all x1, blocking collectives, to_rows(): lax.all_to_all(columns.astype(wire), 'seq', split_axis=2, concat_axis=1,...  8.76 us
    ppermute x6, starting transfers between devices, panel_reduce_scatter(): lax.ppermute(sent, 'panel', [(i, (i + k) % count) for i in range(count)])  8.35 us
    ppermute x2, starting transfers between devices, shifted(): lax.ppermute(value, axis, [(source, source + steps) for source in range(i...  7.48 us
    ppermute x6, starting transfers between devices, panel_parts(): lax.ppermute(value, 'panel', [(i, (i + k) % count) for i in range(count)])  5.84 us
  transfers between devices with their start and end apart: 28, of which 14 were waited for; matrix products, arithmetic and copies ran while one was open for 20% of the time, Pallas kernels for 0%

profile of v1, /device:TPU:9, one launch (start us, length us, event | category | flops | bytes accessed | tf_op | source)
XLA Modules:
  0.0 131.9 jit_solution(10498507975092859598)
XLA Ops:
  0.7 1.3 %collective-permute-start = (bf16[256,256]{1,0:T(8,128)(2,1)}, bf16[256,256]{1,0:T(8,128)(2,1)}, u32[]{:S(2)}, u32[]{:S(2)}) collective-permute-start(bf16[256,256]{1,0:T(8,128)(2,1)} %param.11), channel_id=1, source_target_pairs={{0,1},{1,2},{2,3},{3,0},{4,5},{5,6},{6,7},{7,4},{8,9},{9,10},{10,1... | collective-permute-start | bytes 393224 | tf_op jit(solution)/shard_map/ppermute | solution.py:47
  2.2 2.3 %collective-permute-start.1 = (bf16[256,256]{1,0:T(8,128)(2,1)}, bf16[256,256]{1,0:T(8,128)(2,1)}, u32[]{:S(2)}, u32[]{:S(2)}) collective-permute-start(bf16[256,256]{1,0:T(8,128)(2,1)} %param.11), channel_id=1, source_target_pairs={{0,2},{1,3},{2,0},{3,1},{4,6},{5,7},{6,4},{7,5},{8,10},{9,11},{10,... | collective-permute-start | bytes 393224 | tf_op jit(solution)/shard_map/ppermute | solution.py:47
  4.5 1.0 collective-permute-start.4
  5.5 1.1 copy.36
  6.6 1.6 %collective-permute-start.14 = (f32[1,32,256]{2,1,0:T(8,128)S(1)}, f32[1,32,256]{2,1,0:T(8,128)}, u32[]{:S(2)}, u32[]{:S(2)}) collective-permute-start(f32[1,32,256]{2,1,0:T(8,128)S(1)} %get-tuple-element.26), channel_id=1, source_target_pairs={{0,4},{4,0},{8,12},{12,8},{16,20},{20,16},{24,28},{28,24},{1,5},{5... | collective-permute-start | bytes 98312 | tf_op jit(solution)/shard_map/ppermute | solution.py:31
  8.8 1.0 fusion.86
  9.8 1.0 fusion.84
  10.8 1.3 %slice_bitcast_fusion.5 = (f32[3,256]{1,0:T(4,128)}, f32[3,256]{1,0:T(4,128)}, f32[3,256]{1,0:T(4,128)}) fusion(f32[3,3,256]{2,1,0:T(4,128)} %param.14), kind=kLoop, calls=%fused_computation.185 | loop fusion | bytes 18432 | tf_op jit(solution)/shard_map/mul | solution.py:175
  12.1 1.9 %fusion.96 = f32[256,256]{0,1:T(8,128)} fusion(bf16[256,256]{1,0:T(8,128)(2,1)} %param.12, bf16[256,1024]{1,0:T(8,128)(2,1)} %param.17, s32[]{:T(128)S(6)} %select_n.128), kind=kOutput, calls=%fused_computation.134 | convolution fusion | flops 33554432 | bytes 524292 | tf_op jit(solution)/shard_map/dot_general | solution.py:166
  14.1 1.2 fusion.51
  15.3 0.9 maximum_bitcast_fusion.2
  16.9 1.4 %collective-permute-start.15 = (f32[1,32,256]{2,1,0:T(8,128)S(1)}, f32[1,32,256]{2,1,0:T(8,128)S(1)}, u32[]{:S(2)}, u32[]{:S(2)}) collective-permute-start(f32[1,32,256]{2,1,0:T(8,128)S(1)} %get-tuple-element.25), channel_id=1, source_target_pairs={{0,8},{4,12},{8,0},{12,4},{16,24},{20,28},{24,16},{28,20},{1,9},{5... | collective-permute-start | bytes 98312 | tf_op jit(solution)/shard_map/ppermute | solution.py:31
  18.3 0.8 constant_dynamic-update-slice_fusion.14
  19.7 2.4 %collective-permute-start.16 = (f32[1,32,256]{2,1,0:T(8,128)S(1)}, f32[1,32,256]{2,1,0:T(8,128)S(1)}, u32[]{:S(2)}, u32[]{:S(2)}) collective-permute-start(f32[1,32,256]{2,1,0:T(8,128)S(1)} %get-tuple-element.24), channel_id=1, source_target_pairs={{0,12},{4,8},{8,4},{12,0},{16,28},{20,24},{24,20},{28,16},{1,13},{... | collective-permute-start | bytes 98312 | tf_op jit(solution)/shard_map/ppermute | solution.py:31
  22.1 1.8 %collective-permute-done.16 = f32[1,32,256]{2,1,0:T(8,128)S(1)} collective-permute-done((f32[1,32,256]{2,1,0:T(8,128)S(1)}, f32[1,32,256]{2,1,0:T(8,128)S(1)}, u32[]{:S(2)}, u32[]{:S(2)}) %collective-permute-start.16) | collective-permute-done | bytes 32800 | tf_op jit(solution)/shard_map/ppermute | solution.py:31
  24.0 1.6 %collective-permute-start.17 = (f32[1,32,256]{2,1,0:T(8,128)S(1)}, f32[1,32,256]{2,1,0:T(8,128)S(1)}, u32[]{:S(2)}, u32[]{:S(2)}) collective-permute-start(f32[1,32,256]{2,1,0:T(8,128)S(1)} %get-tuple-element.23), channel_id=1, source_target_pairs={{0,16},{4,20},{8,24},{12,28},{16,0},{20,4},{24,8},{28,12},{1,17},{... | collective-permute-start | bytes 98312 | tf_op jit(solution)/shard_map/ppermute | solution.py:31
  25.5 1.3 collective-permute-done.17
  26.8 2.9 %collective-permute-start.18 = (f32[1,32,256]{2,1,0:T(8,128)S(1)}, f32[1,32,256]{2,1,0:T(8,128)S(1)}, u32[]{:S(2)}, u32[]{:S(2)}) collective-permute-start(f32[1,32,256]{2,1,0:T(8,128)S(1)} %get-tuple-element.22), channel_id=1, source_target_pairs={{0,20},{4,16},{8,28},{12,24},{16,4},{20,0},{24,12},{28,8},{1,21},{... | collective-permute-start | bytes 98312 | tf_op jit(solution)/shard_map/ppermute | solution.py:31
  29.7 1.6 %collective-permute-done.18 = f32[1,32,256]{2,1,0:T(8,128)S(1)} collective-permute-done((f32[1,32,256]{2,1,0:T(8,128)S(1)}, f32[1,32,256]{2,1,0:T(8,128)S(1)}, u32[]{:S(2)}, u32[]{:S(2)}) %collective-permute-start.18) | collective-permute-done | bytes 32800 | tf_op jit(solution)/shard_map/ppermute | solution.py:31
  31.3 0.8 collective-permute-start.19
  32.2 2.8 %collective-permute-done.19 = f32[1,32,256]{2,1,0:T(8,128)S(1)} collective-permute-done((f32[1,32,256]{2,1,0:T(8,128)S(1)}, f32[1,32,256]{2,1,0:T(8,128)S(1)}, u32[]{:S(2)}, u32[]{:S(2)}) %collective-permute-start.19) | collective-permute-done | bytes 32800 | tf_op jit(solution)/shard_map/ppermute | solution.py:31
  35.0 3.5 %collective-permute-start.20 = (f32[1,32,256]{2,1,0:T(8,128)S(1)}, f32[1,32,256]{2,1,0:T(8,128)S(1)}, u32[]{:S(2)}, u32[]{:S(2)}) collective-permute-start(f32[1,32,256]{2,1,0:T(8,128)S(1)} %get-tuple-element.20), channel_id=1, source_target_pairs={{0,28},{4,24},{8,20},{12,16},{16,12},{20,8},{24,4},{28,0},{1,29},{... | collective-permute-start | bytes 98312 | tf_op jit(solution)/shard_map/ppermute | solution.py:31
  38.5 2.0 %collective-permute-done.20 = f32[1,32,256]{2,1,0:T(8,128)S(1)} collective-permute-done((f32[1,32,256]{2,1,0:T(8,128)S(1)}, f32[1,32,256]{2,1,0:T(8,128)S(1)}, u32[]{:S(2)}, u32[]{:S(2)}) %collective-permute-start.20) | collective-permute-done | bytes 32800 | tf_op jit(solution)/shard_map/ppermute | solution.py:31
  42.2 0.8 copy-done.3
  42.9 1.4 %convolution_bitcast_fusion.1 = f32[1,32,2,2,8,256]{5,1,4,2,0,3:T(8,128)S(1)} fusion(f32[32,2,2,8,256]{4,3,2,1,0:T(8,128)S(1)} %maximum_bitcast_fusion.1, f32[1,256,2,256]{3,1,0,2:T(8,128)S(1)} %copy-done.3, f32[1,256,2,256]{3,1,0,2:T(8,128)S(1)} %get-tuple-element.28), kind=kOutput, calls=%fused_computation.17 | convolution fusion | flops 805568512 | bytes 3145728 | tf_op jit(solution)/shard_map/bcerkm,rmsq->bceskq/dot_general | solution.py:139
  44.4 0.9 collective-permute-start.5
  45.2 1.2 convolution_add_fusion.1
  46.5 1.2 fusion.44
  47.7 1.2 fusion.21
  49.0 4.3 %collective-permute-start.3 = (bf16[3,2,256]{2,1,0:T(2,128)(2,1)S(1)}, bf16[3,2,256]{2,1,0:T(2,128)(2,1)S(1)}, u32[]{:S(2)}, u32[]{:S(2)}) collective-permute-start(bf16[3,2,256]{2,1,0:T(2,128)(2,1)S(1)} %slice.115), channel_id=1, source_target_pairs={{0,4},{4,8},{8,12},{12,16},{16,20},{20,24},{24,28},{1,5},{5,9},{9,... | collective-permute-start | bytes 9224 | tf_op jit(solution)/shard_map/ppermute | solution.py:39
  53.3 1.1 convolution_add_fusion.3
  55.7 0.7 maximum_bitcast_fusion.4
  56.5 1.8 %copy.33 = bf16[2,256,256]{2,1,0:T(8,128)(2,1)} copy(bf16[2,256,256]{1,2,0:T(8,128)(2,1)} %maximum_bitcast_fusion.4) | data formatting | bytes 524288 | tf_op jit(solution)/shard_map/convert_element_type | solution.py:121
  58.3 0.9 dynamic-slice_bitcast_fusion.7
  59.2 1.4 %constant_dynamic-update-slice_fusion.7 = bf16[8,2,32,256]{3,2,1,0:T(8,128)(2,1)} fusion(bf16[2,8,32,256]{3,2,1,0:T(8,128)(2,1)} %bitcast.271, s32[]{:T(128)S(6)} %select_n.135), kind=kLoop, calls=%fused_computation.143 | loop fusion | bytes 65540
  60.6 1.5 %collective-permute-start.13 = (bf16[2,32,256]{2,1,0:T(8,128)(2,1)S(1)}, bf16[2,32,256]{2,1,0:T(8,128)(2,1)S(1)}, u32[]{:S(2)}, u32[]{:S(2)}) collective-permute-start(bf16[2,32,256]{2,1,0:T(8,128)(2,1)S(1)} %get-tuple-element.30), channel_id=1, source_target_pairs={{0,28},{4,24},{8,20},{12,16},{16,12},{20,8},{24,4},{28,0},{1,29},{... | collective-permute-start | bytes 98312 | tf_op jit(solution)/shard_map/ppermute | solution.py:31
  62.2 1.2 collective-permute-start.12
  63.4 2.1 %collective-permute-start.11 = (bf16[2,32,256]{2,1,0:T(8,128)(2,1)S(1)}, bf16[2,32,256]{2,1,0:T(8,128)(2,1)S(1)}, u32[]{:S(2)}, u32[]{:S(2)}) collective-permute-start(bf16[2,32,256]{2,1,0:T(8,128)(2,1)S(1)} %get-tuple-element.32), channel_id=1, source_target_pairs={{0,20},{4,16},{8,28},{12,24},{16,4},{20,0},{24,12},{28,8},{1,21},{... | collective-permute-start | bytes 98312 | tf_op jit(solution)/shard_map/ppermute | solution.py:31
  65.5 0.8 collective-permute-start.8
  66.9 1.7 %collective-permute-done.8 = bf16[2,32,256]{2,1,0:T(8,128)(2,1)S(1)} collective-permute-done((bf16[2,32,256]{2,1,0:T(8,128)(2,1)S(1)}, bf16[2,32,256]{2,1,0:T(8,128)(2,1)S(1)}, u32[]{:S(2)}, u32[]{:S(2)}) %collective-permute-start.8) | collective-permute-done | bytes 32800 | tf_op jit(solution)/shard_map/ppermute | solution.py:31
  68.5 2.0 %collective-permute-start.9 = (bf16[2,32,256]{2,1,0:T(8,128)(2,1)S(1)}, bf16[2,32,256]{2,1,0:T(8,128)(2,1)S(1)}, u32[]{:S(2)}, u32[]{:S(2)}) collective-permute-start(bf16[2,32,256]{2,1,0:T(8,128)(2,1)S(1)} %get-tuple-element.34), channel_id=1, source_target_pairs={{0,12},{4,8},{8,4},{12,0},{16,28},{20,24},{24,20},{28,16},{1,13},{... | collective-permute-start | bytes 98312 | tf_op jit(solution)/shard_map/ppermute | solution.py:31
  71.1 1.4 %collective-permute-done.9 = bf16[2,32,256]{2,1,0:T(8,128)(2,1)S(1)} collective-permute-done((bf16[2,32,256]{2,1,0:T(8,128)(2,1)S(1)}, bf16[2,32,256]{2,1,0:T(8,128)(2,1)S(1)}, u32[]{:S(2)}, u32[]{:S(2)}) %collective-permute-start.9) | collective-permute-done | bytes 32800 | tf_op jit(solution)/shard_map/ppermute | solution.py:31
  75.5 2.4 %gather_fusion = bf16[8,2,32,256]{3,2,1,0:T(8,128)(2,1)} fusion(bf16[8,2,32,256]{3,2,1,0:T(8,128)(2,1)} %constant_dynamic-update-slice_fusion, s32[1024]{0:T(1024)} %copy-done.25), kind=kCustom, calls=%fused_computation | custom fusion | bytes 524320 | tf_op jit(solution)/shard_map/gather | solution.py:32
  77.9 1.6 %convolution_bitcast_fusion = f32[2,32,2,2,8,256]{5,4,3,2,1,0:T(8,128)S(1)} fusion(f32[2,2,8,8,1,1]{3,2,1,0,5,4:T(8,128)S(1)} %copy-done.23, bf16[2,32,8,256,1,1]{3,1,0,2,5,4:T(8,128)(2,1)} %bitcast.268), kind=kOutput, calls=%fused_computation.16 | convolution fusion | flops 25165824 | bytes 2360320 | tf_op jit(solution)/shard_map/erkp,bcpm->bcerkm/dot_general | solution.py:137
  80.1 0.8 copy-done.2
  81.1 2.7 %fusion.10 = f32[2,32,2,2,8,256]{5,1,4,2,0,3:T(8,128)S(1)} fusion(f32[2,32,2,2,8,256]{5,4,3,2,1,0:T(8,128)S(1)} %pad_maximum_fusion, f32[1,256,2,256]{3,1,0,2:T(8,128)S(1)} %copy-done.4, f32[1,256,2,256]{3,1,0,2:T(8,128)S(1)} %copy-done.2), kind=kOutput, calls=%fused_computation.14 | convolution fusion | flops 1610874880 | bytes 5242880 | tf_op jit(solution)/shard_map/bcerkm,rmsq->bceskq/dot_general | solution.py:139
  84.4 2.7 %fusion.13 = f32[2,32,2,2,8,256]{5,4,3,2,1,0:T(8,128)S(1)} fusion(f32[2,32,2,2,8,256,1]{5,1,4,2,0,3,6:T(8,128)S(1)} %maximum_bitcast_fusion, f32[1,256,2,256]{3,1,0,2:T(8,128)S(1)} %copy-done.4, f32[1,256,2,256]{3,1,0,2:T(8,128)S(1)} %copy-done.2), kind=kOutput, calls=%fused_computation.15 | convolution fusion | flops 1610874880 | bytes 5242880 | tf_op jit(solution)/shard_map/bceskq,rmsq->bcerkm/dot_general | solution.py:144
  88.6 8.8 %all_to_all.4 = bf16[2,32,8,256]{3,1,0,2:T(8,128)(2,1)S(1)} all-to-all(bf16[2,32,8,256]{3,1,0,2:T(8,128)(2,1)S(1)} %copy.42), channel_id=1, replica_groups=mesh['seq'=8,'panel'=4] {'seq'}, dimensions={2} | all-to-all | bytes 524288 | tf_op jit(solution)/shard_map/all_to_all | solution.py:129
  97.4 0.9 bitcast_convert_fusion
  98.2 1.2 copy.44
  99.7 0.8 copy-done.9
  101.0 3.1 %collective-permute-start.24 = (f32[3,2,256]{2,1,0:T(2,128)S(1)}, f32[3,2,256]{2,1,0:T(2,128)S(1)}, u32[]{:S(2)}, u32[]{:S(2)}) collective-permute-start(f32[3,2,256]{2,1,0:T(2,128)S(1)} %slice.136), channel_id=1, source_target_pairs={{4,0},{8,4},{12,8},{16,12},{20,16},{24,20},{28,24},{5,1},{9,5},{13... | collective-permute-start | bytes 18440 | tf_op jit(solution)/shard_map/ppermute | solution.py:39
  104.3 2.7 %collective-permute-start.21 = (bf16[256,256]{1,0:T(8,128)(2,1)S(1)}, bf16[256,256]{1,0:T(8,128)(2,1)S(1)}, u32[]{:S(2)}, u32[]{:S(2)}) collective-permute-start(bf16[256,256]{1,0:T(8,128)(2,1)S(1)} %convolution_convert_fusion.2), channel_id=1, source_target_pairs={{0,1},{1,2},{2,3},{3,0},{4,5},{5,6},{6,7},{7,4},{8,9},{9,10},{10,1... | collective-permute-start | bytes 393224 | tf_op jit(solution)/shard_map/ppermute | solution.py:58
  107.0 1.0 collective-permute-start.22
  109.3 1.2 collective-permute-start.25
  110.5 3.2 %collective-permute-start.26 = (bf16[256,256]{1,0:T(8,128)(2,1)S(1)}, bf16[256,256]{1,0:T(8,128)(2,1)S(1)}, u32[]{:S(2)}, u32[]{:S(2)}) collective-permute-start(bf16[256,256]{1,0:T(8,128)(2,1)S(1)} %fusion.31), channel_id=1, source_target_pairs={{0,2},{1,3},{2,0},{3,1},{4,6},{5,7},{6,4},{7,5},{8,10},{9,11},{10,... | collective-permute-start | bytes 393224 | tf_op jit(solution)/shard_map/ppermute | solution.py:58
  114.0 1.9 %collective-permute-done.21 = bf16[256,256]{1,0:T(8,128)(2,1)S(1)} collective-permute-done((bf16[256,256]{1,0:T(8,128)(2,1)S(1)}, bf16[256,256]{1,0:T(8,128)(2,1)S(1)}, u32[]{:S(2)}, u32[]{:S(2)}) %collective-permute-start.21) | collective-permute-done | bytes 131104 | tf_op jit(solution)/shard_map/ppermute | solution.py:58
  116.0 8.4 %collective-permute-done.22 = bf16[256,256]{1,0:T(8,128)(2,1)S(1)} collective-permute-done((bf16[256,256]{1,0:T(8,128)(2,1)S(1)}, bf16[256,256]{1,0:T(8,128)(2,1)S(1)}, u32[]{:S(2)}, u32[]{:S(2)}) %collective-permute-start.22) | collective-permute-done | bytes 131104 | tf_op jit(solution)/shard_map/ppermute | solution.py:58
  124.4 0.9 collective-permute-done.23
  125.3 0.9 add_convert_fusion
  126.2 1.0 collective-permute-done.25
  127.2 2.7 %collective-permute-done.26 = bf16[256,256]{1,0:T(8,128)(2,1)S(1)} collective-permute-done((bf16[256,256]{1,0:T(8,128)(2,1)S(1)}, bf16[256,256]{1,0:T(8,128)(2,1)S(1)}, u32[]{:S(2)}, u32[]{:S(2)}) %collective-permute-start.26) | collective-permute-done | bytes 131104 | tf_op jit(solution)/shard_map/ppermute | solution.py:58
  129.9 1.0 collective-permute-done.27
  130.9 1.0 fusion.62
  (118 shorter events, 14.4 us)
Async XLA Ops:
  0.6 13.4 %copy-start = (bf16[3,1024,256]{2,1,0:T(8,128)(2,1)S(1)}, bf16[3,1024,256]{2,1,0:T(8,128)(2,1)}, u32[]{:S(2)}) copy-start(bf16[3,1024,256]{2,1,0:T(8,128)(2,1)} %param.13) | copy-start | bytes 4718596
  0.6 13.4 %copy-start.12 = (bf16[256,256]{1,0:T(8,128)(2,1)S(1)}, bf16[256,256]{1,0:T(8,128)(2,1)}, u32[]{:S(2)}) copy-start(bf16[256,256]{1,0:T(8,128)(2,1)} %param.11) | copy-start | bytes 393220
  0.7 43.7 %collective-permute-start = (bf16[256,256]{1,0:T(8,128)(2,1)}, bf16[256,256]{1,0:T(8,128)(2,1)}, u32[]{:S(2)}, u32[]{:S(2)}) collective-permute-start(bf16[256,256]{1,0:T(8,128)(2,1)} %param.11), channel_id=1, source_target_pairs={{0,1},{1,2},{2,3},{3,0},{4,5},{5,6},{6,7},{7,4},{8,9},{9,10},{10,1... | collective-permute-start | bytes 393224 | tf_op jit(solution)/shard_map/ppermute | solution.py:47
  2.0 44.4 %collective-permute-start.2 = (bf16[256,256]{1,0:T(8,128)(2,1)}, bf16[256,256]{1,0:T(8,128)(2,1)}, u32[]{:S(2)}, u32[]{:S(2)}) collective-permute-start(bf16[256,256]{1,0:T(8,128)(2,1)} %param.11), channel_id=1, source_target_pairs={{0,3},{1,0},{2,1},{3,2},{4,7},{5,4},{6,5},{7,6},{8,11},{9,8},{10,9... | collective-permute-start | bytes 393224 | tf_op jit(solution)/shard_map/ppermute | solution.py:47
  2.2 45.5 %collective-permute-start.1 = (bf16[256,256]{1,0:T(8,128)(2,1)}, bf16[256,256]{1,0:T(8,128)(2,1)}, u32[]{:S(2)}, u32[]{:S(2)}) collective-permute-start(bf16[256,256]{1,0:T(8,128)(2,1)} %param.11), channel_id=1, source_target_pairs={{0,2},{1,3},{2,0},{3,1},{4,6},{5,7},{6,4},{7,5},{8,10},{9,11},{10,... | collective-permute-start | bytes 393224 | tf_op jit(solution)/shard_map/ppermute | solution.py:47
  4.5 48.8 %collective-permute-start.4 = (bf16[256,256]{1,0:T(8,128)(2,1)}, bf16[256,256]{1,0:T(8,128)(2,1)}, u32[]{:S(2)}, u32[]{:S(2)}) collective-permute-start(bf16[256,256]{1,0:T(8,128)(2,1)} %param.12), channel_id=1, source_target_pairs={{0,1},{1,2},{2,3},{3,0},{4,5},{5,6},{6,7},{7,4},{8,9},{9,10},{10,1... | collective-permute-start | bytes 393224 | tf_op jit(solution)/shard_map/ppermute | solution.py:47
  6.6 10.2 %collective-permute-start.14 = (f32[1,32,256]{2,1,0:T(8,128)S(1)}, f32[1,32,256]{2,1,0:T(8,128)}, u32[]{:S(2)}, u32[]{:S(2)}) collective-permute-start(f32[1,32,256]{2,1,0:T(8,128)S(1)} %get-tuple-element.26), channel_id=1, source_target_pairs={{0,4},{4,0},{8,12},{12,8},{16,20},{20,16},{24,28},{28,24},{1,5},{5... | collective-permute-start | bytes 98312 | tf_op jit(solution)/shard_map/ppermute | solution.py:31
  14.1 27.2 %copy-start.24 = (f32[2,2,8,8,1]{3,2,1,0,4:T(8,128)S(1)}, f32[2,2,8,8,1]{3,2,1,0,4:T(8,128)}, u32[]{:S(2)}) copy-start(f32[2,2,8,8,1]{3,2,1,0,4:T(8,128)} %constant.108) | copy-start | bytes 3076
  15.3 26.6 %copy-start.11 = (f32[2,8,256]{2,1,0:T(8,128)S(1)}, f32[2,8,256]{2,1,0:T(8,128)}, u32[]{:S(2)}) copy-start(f32[2,8,256]{2,1,0:T(8,128)} %constant.103.clone) | copy-start | bytes 49156
  15.3 26.6 %copy-start.13 = (f32[2,8,256]{2,1,0:T(8,128)S(1)}, f32[2,8,256]{2,1,0:T(8,128)}, u32[]{:S(2)}) copy-start(f32[2,8,256]{2,1,0:T(8,128)} %constant.104.clone) | copy-start | bytes 49156
  16.2 26.0 %copy-start.1 = (f32[1,256,2,256]{3,1,0,2:T(8,128)}, f32[1,256,2,256]{3,1,0,2:T(8,128)S(1)}, u32[]{:S(2)}) copy-start(f32[1,256,2,256]{3,1,0,2:T(8,128)S(1)} %get-tuple-element.28) | copy-start | bytes 1572868
  16.9 25.2 %copy-start.25 = (s32[1024]{0:T(1024)}, s32[1024]{0:T(1024)S(1)}, u32[]{:S(2)}) copy-start(s32[1024]{0:T(1024)S(1)} %pad_clamp_fusion) | copy-start | bytes 12292
  16.9 2.8 %collective-permute-start.15 = (f32[1,32,256]{2,1,0:T(8,128)S(1)}, f32[1,32,256]{2,1,0:T(8,128)S(1)}, u32[]{:S(2)}, u32[]{:S(2)}) collective-permute-start(f32[1,32,256]{2,1,0:T(8,128)S(1)} %get-tuple-element.25), channel_id=1, source_target_pairs={{0,8},{4,12},{8,0},{12,4},{16,24},{20,28},{24,16},{28,20},{1,9},{5... | collective-permute-start | bytes 98312 | tf_op jit(solution)/shard_map/ppermute | solution.py:31
  19.7 4.3 %collective-permute-start.16 = (f32[1,32,256]{2,1,0:T(8,128)S(1)}, f32[1,32,256]{2,1,0:T(8,128)S(1)}, u32[]{:S(2)}, u32[]{:S(2)}) collective-permute-start(f32[1,32,256]{2,1,0:T(8,128)S(1)} %get-tuple-element.24), channel_id=1, source_target_pairs={{0,12},{4,8},{8,4},{12,0},{16,28},{20,24},{24,20},{28,16},{1,13},{... | collective-permute-start | bytes 98312 | tf_op jit(solution)/shard_map/ppermute | solution.py:31
  24.0 2.9 %collective-permute-start.17 = (f32[1,32,256]{2,1,0:T(8,128)S(1)}, f32[1,32,256]{2,1,0:T(8,128)S(1)}, u32[]{:S(2)}, u32[]{:S(2)}) collective-permute-start(f32[1,32,256]{2,1,0:T(8,128)S(1)} %get-tuple-element.23), channel_id=1, source_target_pairs={{0,16},{4,20},{8,24},{12,28},{16,0},{20,4},{24,8},{28,12},{1,17},{... | collective-permute-start | bytes 98312 | tf_op jit(solution)/shard_map/ppermute | solution.py:31
  26.8 4.5 %collective-permute-start.18 = (f32[1,32,256]{2,1,0:T(8,128)S(1)}, f32[1,32,256]{2,1,0:T(8,128)S(1)}, u32[]{:S(2)}, u32[]{:S(2)}) collective-permute-start(f32[1,32,256]{2,1,0:T(8,128)S(1)} %get-tuple-element.22), channel_id=1, source_target_pairs={{0,20},{4,16},{8,28},{12,24},{16,4},{20,0},{24,12},{28,8},{1,21},{... | collective-permute-start | bytes 98312 | tf_op jit(solution)/shard_map/ppermute | solution.py:31
  31.3 3.7 %collective-permute-start.19 = (f32[1,32,256]{2,1,0:T(8,128)S(1)}, f32[1,32,256]{2,1,0:T(8,128)S(1)}, u32[]{:S(2)}, u32[]{:S(2)}) collective-permute-start(f32[1,32,256]{2,1,0:T(8,128)S(1)} %get-tuple-element.21), channel_id=1, source_target_pairs={{0,24},{4,28},{8,16},{12,20},{16,8},{20,12},{24,0},{28,4},{1,25},{... | collective-permute-start | bytes 98312 | tf_op jit(solution)/shard_map/ppermute | solution.py:31
  35.0 5.5 %collective-permute-start.20 = (f32[1,32,256]{2,1,0:T(8,128)S(1)}, f32[1,32,256]{2,1,0:T(8,128)S(1)}, u32[]{:S(2)}, u32[]{:S(2)}) collective-permute-start(f32[1,32,256]{2,1,0:T(8,128)S(1)} %get-tuple-element.20), channel_id=1, source_target_pairs={{0,28},{4,24},{8,20},{12,16},{16,12},{20,8},{24,4},{28,0},{1,29},{... | collective-permute-start | bytes 98312 | tf_op jit(solution)/shard_map/ppermute | solution.py:31
  40.5 14.0 %collective-permute-start.6 = (bf16[256,256]{1,0:T(8,128)(2,1)}, bf16[256,256]{1,0:T(8,128)(2,1)S(1)}, u32[]{:S(2)}, u32[]{:S(2)}) collective-permute-start(bf16[256,256]{1,0:T(8,128)(2,1)} %param.12), channel_id=1, source_target_pairs={{0,3},{1,0},{2,1},{3,2},{4,7},{5,4},{6,5},{7,6},{8,11},{9,8},{10,9... | collective-permute-start | bytes 393224 | tf_op jit(solution)/shard_map/ppermute | solution.py:47
  41.9 1.0 copy-start.3
  42.9 2.3 %copy-start.5 = (f32[3,256,256]{1,2,0:T(8,128)S(1)}, f32[3,256,256]{1,2,0:T(8,128)}, u32[]{:S(2)}) copy-start(f32[3,256,256]{1,2,0:T(8,128)} %fusion.51) | copy-start | bytes 2359300
  44.4 10.3 %collective-permute-start.5 = (bf16[256,256]{1,0:T(8,128)(2,1)}, bf16[256,256]{1,0:T(8,128)(2,1)S(1)}, u32[]{:S(2)}, u32[]{:S(2)}) collective-permute-start(bf16[256,256]{1,0:T(8,128)(2,1)} %param.12), channel_id=1, source_target_pairs={{0,2},{1,3},{2,0},{3,1},{4,6},{5,7},{6,4},{7,5},{8,10},{9,11},{10,... | collective-permute-start | bytes 393224 | tf_op jit(solution)/shard_map/ppermute | solution.py:47
  46.4 6.9 %copy-start.8 = (bf16[256,1024]{1,0:T(8,128)(2,1)S(1)}, bf16[256,1024]{1,0:T(8,128)(2,1)}, u32[]{:S(2)}) copy-start(bf16[256,1024]{1,0:T(8,128)(2,1)} %param.17) | copy-start | bytes 1572868
  46.4 6.9 %copy-start.10 = (f32[256,256]{0,1:T(8,128)S(1)}, f32[256,256]{0,1:T(8,128)}, u32[]{:S(2)}) copy-start(f32[256,256]{0,1:T(8,128)} %fusion.96) | copy-start | bytes 786436
  48.9 6.2 %copy-start.15 = (f32[3,256]{1,0:T(4,128)S(1)}, f32[3,256]{1,0:T(4,128)}, u32[]{:S(2)}) copy-start(f32[3,256]{1,0:T(4,128)} %get-tuple-element.37) | copy-start | bytes 9220
  48.9 6.2 %copy-start.17 = (f32[3,256]{1,0:T(4,128)S(1)}, f32[3,256]{1,0:T(4,128)}, u32[]{:S(2)}) copy-start(f32[3,256]{1,0:T(4,128)} %get-tuple-element.38) | copy-start | bytes 9220
  48.9 6.2 %copy-start.19 = (f32[3,256]{1,0:T(4,128)S(1)}, f32[3,256]{1,0:T(4,128)}, u32[]{:S(2)}) copy-start(f32[3,256]{1,0:T(4,128)} %get-tuple-element.39) | copy-start | bytes 9220
  49.0 6.0 %collective-permute-start.3 = (bf16[3,2,256]{2,1,0:T(2,128)(2,1)S(1)}, bf16[3,2,256]{2,1,0:T(2,128)(2,1)S(1)}, u32[]{:S(2)}, u32[]{:S(2)}) collective-permute-start(bf16[3,2,256]{2,1,0:T(2,128)(2,1)S(1)} %slice.115), channel_id=1, source_target_pairs={{0,4},{4,8},{8,12},{12,16},{16,20},{20,24},{24,28},{1,5},{5,9},{9,... | collective-permute-start | bytes 9224 | tf_op jit(solution)/shard_map/ppermute | solution.py:39
  55.0 0.7 copy-start.6
  55.4 22.5 %copy-start.23 = (f32[2,2,8,8,1,1]{3,2,1,0,5,4:T(8,128)S(1)}, f32[2,2,8,8,1,1]{3,2,1,0,5,4:T(8,128)}, u32[]{:S(2)}) copy-start(f32[2,2,8,8,1,1]{3,2,1,0,5,4:T(8,128)} %constant.107) | copy-start | bytes 3076
  56.5 23.1 %copy-start.14 = (f32[2,8,256]{2,1,0:T(8,128)S(1)}, f32[2,8,256]{2,1,0:T(8,128)}, u32[]{:S(2)}) copy-start(f32[2,8,256]{2,1,0:T(8,128)} %constant.104.clone) | copy-start | bytes 49156
  59.2 6.3 %collective-permute-start.7 = (bf16[2,32,256]{2,1,0:T(8,128)(2,1)S(1)}, bf16[2,32,256]{2,1,0:T(8,128)(2,1)S(1)}, u32[]{:S(2)}, u32[]{:S(2)}) collective-permute-start(bf16[2,32,256]{2,1,0:T(8,128)(2,1)S(1)} %get-tuple-element.36), channel_id=1, source_target_pairs={{0,4},{4,0},{8,12},{12,8},{16,20},{20,16},{24,28},{28,24},{1,5},{5... | collective-permute-start | bytes 98312 | tf_op jit(solution)/shard_map/ppermute | solution.py:31
  60.6 14.3 %collective-permute-start.13 = (bf16[2,32,256]{2,1,0:T(8,128)(2,1)S(1)}, bf16[2,32,256]{2,1,0:T(8,128)(2,1)S(1)}, u32[]{:S(2)}, u32[]{:S(2)}) collective-permute-start(bf16[2,32,256]{2,1,0:T(8,128)(2,1)S(1)} %get-tuple-element.30), channel_id=1, source_target_pairs={{0,28},{4,24},{8,20},{12,16},{16,12},{20,8},{24,4},{28,0},{1,29},{... | collective-permute-start | bytes 98312 | tf_op jit(solution)/shard_map/ppermute | solution.py:31
  62.2 12.2 %collective-permute-start.12 = (bf16[2,32,256]{2,1,0:T(8,128)(2,1)S(1)}, bf16[2,32,256]{2,1,0:T(8,128)(2,1)S(1)}, u32[]{:S(2)}, u32[]{:S(2)}) collective-permute-start(bf16[2,32,256]{2,1,0:T(8,128)(2,1)S(1)} %get-tuple-element.31), channel_id=1, source_target_pairs={{0,24},{4,28},{8,16},{12,20},{16,8},{20,12},{24,0},{28,4},{1,25},{... | collective-permute-start | bytes 98312 | tf_op jit(solution)/shard_map/ppermute | solution.py:31
  63.4 10.4 %collective-permute-start.11 = (bf16[2,32,256]{2,1,0:T(8,128)(2,1)S(1)}, bf16[2,32,256]{2,1,0:T(8,128)(2,1)S(1)}, u32[]{:S(2)}, u32[]{:S(2)}) collective-permute-start(bf16[2,32,256]{2,1,0:T(8,128)(2,1)S(1)} %get-tuple-element.32), channel_id=1, source_target_pairs={{0,20},{4,16},{8,28},{12,24},{16,4},{20,0},{24,12},{28,8},{1,21},{... | collective-permute-start | bytes 98312 | tf_op jit(solution)/shard_map/ppermute | solution.py:31
  65.5 7.7 %collective-permute-start.10 = (bf16[2,32,256]{2,1,0:T(8,128)(2,1)S(1)}, bf16[2,32,256]{2,1,0:T(8,128)(2,1)S(1)}, u32[]{:S(2)}, u32[]{:S(2)}) collective-permute-start(bf16[2,32,256]{2,1,0:T(8,128)(2,1)S(1)} %get-tuple-element.33), channel_id=1, source_target_pairs={{0,16},{4,20},{8,24},{12,28},{16,0},{20,4},{24,8},{28,12},{1,17},{... | collective-permute-start | bytes 98312 | tf_op jit(solution)/shard_map/ppermute | solution.py:31
  65.5 3.1 %collective-permute-start.8 = (bf16[2,32,256]{2,1,0:T(8,128)(2,1)S(1)}, bf16[2,32,256]{2,1,0:T(8,128)(2,1)S(1)}, u32[]{:S(2)}, u32[]{:S(2)}) collective-permute-start(bf16[2,32,256]{2,1,0:T(8,128)(2,1)S(1)} %get-tuple-element.35), channel_id=1, source_target_pairs={{0,8},{4,12},{8,0},{12,4},{16,24},{20,28},{24,16},{28,20},{1,9},{5... | collective-permute-start | bytes 98312 | tf_op jit(solution)/shard_map/ppermute | solution.py:31
  68.5 4.0 %collective-permute-start.9 = (bf16[2,32,256]{2,1,0:T(8,128)(2,1)S(1)}, bf16[2,32,256]{2,1,0:T(8,128)(2,1)S(1)}, u32[]{:S(2)}, u32[]{:S(2)}) collective-permute-start(bf16[2,32,256]{2,1,0:T(8,128)(2,1)S(1)} %get-tuple-element.34), channel_id=1, source_target_pairs={{0,12},{4,8},{8,4},{12,0},{16,28},{20,24},{24,20},{28,16},{1,13},{... | collective-permute-start | bytes 98312 | tf_op jit(solution)/shard_map/ppermute | solution.py:31
  79.9 1.0 copy-start.2
  79.9 1.2 copy-start.4
  84.4 2.7 %copy-start.22 = (f32[2,8,256]{2,1,0:T(8,128)S(1)}, f32[2,8,256]{2,1,0:T(8,128)}, u32[]{:S(2)}) copy-start(f32[2,8,256]{2,1,0:T(8,128)} %constant.106) | copy-start | bytes 49156
  87.1 0.7 copy-start.21
  87.9 11.6 %copy-start.7 = (f32[256,256]{1,0:T(8,128)S(1)}, f32[256,256]{1,0:T(8,128)}, u32[]{:S(2)}) copy-start(f32[256,256]{1,0:T(8,128)} %copy-done.6) | copy-start | bytes 786436
  87.9 11.6 %copy-start.26 = (f32[256]{0:T(256)S(1)}, f32[256]{0:T(256)}, u32[]{:S(2)}) copy-start(f32[256]{0:T(256)} %param.15) | copy-start | bytes 3076
  99.5 1.0 copy-start.9
  100.5 7.8 %copy-start.16 = (f32[3,256]{1,0:T(4,128)S(1)}, f32[3,256]{1,0:T(4,128)}, u32[]{:S(2)}) copy-start(f32[3,256]{1,0:T(4,128)} %get-tuple-element.37) | copy-start | bytes 9220
  100.5 7.9 %copy-start.18 = (f32[3,256]{1,0:T(4,128)S(1)}, f32[3,256]{1,0:T(4,128)}, u32[]{:S(2)}) copy-start(f32[3,256]{1,0:T(4,128)} %get-tuple-element.38) | copy-start | bytes 9220
  100.5 7.9 %copy-start.20 = (f32[3,256]{1,0:T(4,128)S(1)}, f32[3,256]{1,0:T(4,128)}, u32[]{:S(2)}) copy-start(f32[3,256]{1,0:T(4,128)} %get-tuple-element.39) | copy-start | bytes 9220
  101.0 7.3 %collective-permute-start.24 = (f32[3,2,256]{2,1,0:T(2,128)S(1)}, f32[3,2,256]{2,1,0:T(2,128)S(1)}, u32[]{:S(2)}, u32[]{:S(2)}) collective-permute-start(f32[3,2,256]{2,1,0:T(2,128)S(1)} %slice.136), channel_id=1, source_target_pairs={{4,0},{8,4},{12,8},{16,12},{20,16},{24,20},{28,24},{5,1},{9,5},{13... | collective-permute-start | bytes 18440 | tf_op jit(solution)/shard_map/ppermute | solution.py:39
  104.3 11.6 %collective-permute-start.21 = (bf16[256,256]{1,0:T(8,128)(2,1)S(1)}, bf16[256,256]{1,0:T(8,128)(2,1)S(1)}, u32[]{:S(2)}, u32[]{:S(2)}) collective-permute-start(bf16[256,256]{1,0:T(8,128)(2,1)S(1)} %convolution_convert_fusion.2), channel_id=1, source_target_pairs={{0,1},{1,2},{2,3},{3,0},{4,5},{5,6},{6,7},{7,4},{8,9},{9,10},{10,1... | collective-permute-start | bytes 393224 | tf_op jit(solution)/shard_map/ppermute | solution.py:58
  107.0 17.4 %collective-permute-start.22 = (bf16[256,256]{1,0:T(8,128)(2,1)S(1)}, bf16[256,256]{1,0:T(8,128)(2,1)S(1)}, u32[]{:S(2)}, u32[]{:S(2)}) collective-permute-start(bf16[256,256]{1,0:T(8,128)(2,1)S(1)} %convolution_convert_fusion.1), channel_id=1, source_target_pairs={{0,2},{1,3},{2,0},{3,1},{4,6},{5,7},{6,4},{7,5},{8,10},{9,11},{10,... | collective-permute-start | bytes 393224 | tf_op jit(solution)/shard_map/ppermute | solution.py:58
  108.0 17.3 %collective-permute-start.23 = (bf16[256,256]{1,0:T(8,128)(2,1)S(1)}, bf16[256,256]{1,0:T(8,128)(2,1)S(1)}, u32[]{:S(2)}, u32[]{:S(2)}) collective-permute-start(bf16[256,256]{1,0:T(8,128)(2,1)S(1)} %convolution_convert_fusion), channel_id=1, source_target_pairs={{0,3},{1,0},{2,1},{3,2},{4,7},{5,4},{6,5},{7,6},{8,11},{9,8},{10,9... | collective-permute-start | bytes 393224 | tf_op jit(solution)/shard_map/ppermute | solution.py:58
  109.3 17.9 %collective-permute-start.25 = (bf16[256,256]{1,0:T(8,128)(2,1)S(1)}, bf16[256,256]{1,0:T(8,128)(2,1)S(1)}, u32[]{:S(2)}, u32[]{:S(2)}) collective-permute-start(bf16[256,256]{1,0:T(8,128)(2,1)S(1)} %fusion.30), channel_id=1, source_target_pairs={{0,1},{1,2},{2,3},{3,0},{4,5},{5,6},{6,7},{7,4},{8,9},{9,10},{10,1... | collective-permute-start | bytes 393224 | tf_op jit(solution)/shard_map/ppermute | solution.py:58
  110.5 19.4 %collective-permute-start.26 = (bf16[256,256]{1,0:T(8,128)(2,1)S(1)}, bf16[256,256]{1,0:T(8,128)(2,1)S(1)}, u32[]{:S(2)}, u32[]{:S(2)}) collective-permute-start(bf16[256,256]{1,0:T(8,128)(2,1)S(1)} %fusion.31), channel_id=1, source_target_pairs={{0,2},{1,3},{2,0},{3,1},{4,6},{5,7},{6,4},{7,5},{8,10},{9,11},{10,... | collective-permute-start | bytes 393224 | tf_op jit(solution)/shard_map/ppermute | solution.py:58
  116.0 15.0 %collective-permute-start.27 = (bf16[256,256]{1,0:T(8,128)(2,1)S(1)}, bf16[256,256]{1,0:T(8,128)(2,1)S(1)}, u32[]{:S(2)}, u32[]{:S(2)}) collective-permute-start(bf16[256,256]{1,0:T(8,128)(2,1)S(1)} %fusion.32), channel_id=1, source_target_pairs={{0,3},{1,0},{2,1},{3,2},{4,7},{5,4},{6,5},{7,6},{8,11},{9,8},{10,9... | collective-permute-start | bytes 393224 | tf_op jit(solution)/shard_map/ppermute | solution.py:58
